TPU v7x, 512 devices: a whole 4x8x8 slice. The times are simulated.
512 devices in a mesh: expert: 64 (over x, z, core), group: 8 (over y).
Axes of the slice: x: 4, y: 8, z: 8, core: 2. Of those that a mesh axis runs over, the one named last changes fastest.
Arguments:
- tokens: bfloat16 [4096, 4096], P('expert', 'group'), may hold values from -6 to 6
- gate_weight: bfloat16 [64, 1536, 4096], P('expert', 'group'), may hold values from -0.09375 to 0.09375
- up_weight: bfloat16 [64, 1536, 4096], P('expert', 'group'), may hold values from -0.09375 to 0.09375
- down_weight: bfloat16 [64, 1536, 4096], P('expert', 'group'), may hold values from -0.15625 to 0.15625
- expert_ids: int32 [4096, 8], P('expert'), may hold values from 0 to 63, all different within a row; in each aligned block of 64 rows (0 to 63, 64 to 127, ...) at most 12 rows name the same one
- gate_scores: bfloat16 [4096, 8], P('expert'), may hold values from 0.19921875 to 1
Outputs:
- mixed: bfloat16 [4096, 4096], P('expert', 'group')
Inputs may be any that keep to these rules, and one draw needn't show every extreme that they name: `expert_ids`: the 8 experts of a token are distinct; within the 64 rows of one device no expert is named by more than 12 rows, a bound that some block reaches.
All inputs are finite; a program needn't handle non-finite values.
Results may differ from a plain program's by a relative error of at most 0.019.
Values may be sent and summed in bfloat16 or wider, within the bound.
No kernel may reach another device: no remote copies, remote signals or barrier semaphores. Data moves between devices by JAX's collectives and lax.ppermute only.
A program may use at most 128 MiB of HBM per device.

v0:
```python
import jax
import jax.numpy as jnp
from jax import lax
from jax.sharding import PartitionSpec as P


def per_device(tokens, gate_weight, up_weight, down_weight, expert_ids, gate_scores):
    experts = lax.axis_size("expert")
    tok_rows = tokens.shape[0]
    top_count = expert_ids.shape[1]
    capacity = tok_rows * top_count * 3 // (2 * experts)
    flat_ids = expert_ids.reshape(-1)
    onehot = (flat_ids[:, None] == jnp.arange(experts, dtype=jnp.int32)[None, :]).astype(jnp.int32)
    before = jnp.cumsum(onehot, axis=0) - onehot
    slot_index = jnp.sum(before * onehot, axis=1).reshape(tok_rows, top_count)
    slot_keys = expert_ids * capacity + slot_index
    columns = jnp.arange(experts * capacity, dtype=jnp.int32)
    matches = slot_keys[:, :, None] == columns[None, None, :]
    selector = jnp.any(matches, axis=1).astype(jnp.bfloat16)
    weights = jnp.sum(
        jnp.where(matches, gate_scores[:, :, None].astype(jnp.float32), 0.0), axis=1
    ).astype(jnp.bfloat16)
    whole_rows = lax.all_gather(tokens, "group", axis=1, tiled=True)
    placed = lax.dot_general(
        selector, whole_rows, (((0,), (0,)), ((), ())), preferred_element_type=jnp.float32
    )
    arrived = lax.all_to_all(
        placed.astype(jnp.bfloat16).reshape(experts, capacity, whole_rows.shape[1]),
        "expert",
        split_axis=0,
        concat_axis=0,
        tiled=True,
    )
    row_block = arrived.reshape(-1, arrived.shape[2])
    gate_value = lax.dot_general(
        row_block, gate_weight[0], (((1,), (1,)), ((), ())), preferred_element_type=jnp.float32
    )
    up_value = lax.dot_general(
        row_block, up_weight[0], (((1,), (1,)), ((), ())), preferred_element_type=jnp.float32
    )
    hidden = (jax.nn.silu(gate_value) * up_value).astype(jnp.bfloat16)
    partial_value = jnp.dot(hidden, down_weight[0], preferred_element_type=jnp.float32)
    returned = lax.all_to_all(
        partial_value.astype(jnp.bfloat16).reshape(arrived.shape),
        "expert",
        split_axis=0,
        concat_axis=0,
        tiled=True,
    )
    combined = jnp.dot(
        weights, returned.reshape(experts * capacity, -1), preferred_element_type=jnp.float32
    )
    return lax.psum_scatter(combined.astype(jnp.bfloat16), "group", scatter_dimension=1, tiled=True)


def solution(mesh):
    placed = (
        P("expert", "group"),
        P("expert", "group", None),
        P("expert", "group", None),
        P("expert", "group", None),
        P("expert", None),
        P("expert", None),
    )
    return jax.shard_map(
        per_device, mesh=mesh, in_specs=placed, out_specs=P("expert", "group"), check_vma=False
    )
```

profile of v0, /device:TPU:2, one launch (start us, length us, event | category | flops | bytes accessed | tf_op | source)
XLA Modules:
  0.0 540.2 jit_solution(18164312794375199998)
XLA Ops:
  6.5 0.0 copy-start
  6.5 0.9 copy.21
  7.4 0.1 eq.42
  7.5 0.1 eq.38
  7.6 1.2 reduce-window.6
  8.8 0.2 slice_reduce_fusion
  9.1 0.1 fusion.22
  9.2 0.1 reshape.36
  9.3 0.1 copy.24
  9.4 0.7 multiply_add_fusion
  10.1 0.1 copy.25
  10.2 0.5 fusion.5
  10.7 27.1 %all_gather.3 = bf16[64,4096]{1,0:T(8,128)(2,1)S(1)} all-gather(bf16[64,512]{1,0:T(8,128)(2,1)} %param.6), channel_id=1, replica_groups=mesh['expert'=64,'group'=8] {'group'}, dimensions={1}, use_global_device_ids=true | all-gather | bytes 589824 | tf_op jit(solution)/shard_map/all_gather | solution.py:23
  37.9 4.6 convolution_convert_fusion
  42.4 9.8 %reshape.37 = bf16[64,12,4096]{2,1,0:T(8,128)(2,1)} reshape(bf16[768,4096]{1,0:T(8,128)(2,1)} %convolution_convert_fusion) | data formatting | bytes 12582912 | tf_op jit(solution)/shard_map/reshape | solution.py:28
  52.2 198.1 %all_to_all.10 = bf16[64,12,4096]{2,1,0:T(8,128)(2,1)} all-to-all(bf16[64,12,4096]{2,1,0:T(8,128)(2,1)} %reshape.37), channel_id=1, replica_groups=mesh['expert'=64,'group'=8] {'expert'}, dimensions={0} | all-to-all | bytes 12582912 | tf_op jit(solution)/shard_map/all_to_all | solution.py:27
  250.3 0.0 copy-start.2
  250.3 10.1 %reshape.38 = bf16[768,4096]{1,0:T(8,128)(2,1)} reshape(bf16[64,12,4096]{2,1,0:T(8,128)(2,1)} %all_to_all.10) | data formatting | bytes 12582912 | tf_op jit(solution)/shard_map/reshape | solution.py:34
  260.4 0.0 copy-done.2
  260.4 5.8 %fusion.3 = f32[768,192]{0,1:T(8,128)} fusion(bf16[768,4096]{1,0:T(8,128)(2,1)} %reshape.38, bf16[1,192,4096]{2,1,0:T(8,128)(2,1)S(1)} %copy-done.2), kind=kOutput, calls=%fused_computation.6 | convolution fusion | flops 1207959552 | bytes 8454144 | tf_op jit(solution)/shard_map/dot_general | solution.py:35
  266.3 0.0 copy-done
  266.3 13.5 %convolution_convert_fusion.1 = bf16[768,4096]{1,0:T(8,128)(2,1)} fusion(bf16[1,192,4096]{2,1,0:T(8,128)(2,1)S(1)} %copy-done, bf16[768,4096]{1,0:T(8,128)(2,1)} %reshape.38, bf16[1,192,4096]{2,1,0:T(8,128)(2,1)} %param.8, f32[768,192]{0,1:T(8,128)} %fusion.3), kind=kOutput, calls=%fused_computation.1 | convolution fusion | flops 2419949568 | bytes 16318464 | tf_op jit(solution)/shard_map/dot_general | solution.py:42
  279.7 9.8 %reshape.39 = bf16[64,12,4096]{2,1,0:T(8,128)(2,1)} reshape(bf16[768,4096]{1,0:T(8,128)(2,1)} %convolution_convert_fusion.1) | data formatting | bytes 12582912 | tf_op jit(solution)/shard_map/reshape | solution.py:44
  289.5 0.0 copy-start.1
  289.5 8.0 %all-to-all-start.1 = ((bf16[64,12,4096]{2,1,0:T(8,128)(2,1)}), bf16[64,12,4096]{2,1,0:T(8,128)(2,1)}, u32[]{:S(2)}, u32[]{:S(2)}) async-start(bf16[64,12,4096]{2,1,0:T(8,128)(2,1)} %reshape.39), calls=%async_computation.1 | async-start | bytes 16777216 | tf_op jit(solution)/shard_map/all_to_all | solution.py:43
  297.6 0.0 reduce-scatter.2.cloned.1.call-start
  297.6 0.0 copy-done.1
  297.6 0.1 copy.26
  297.7 0.6 select_reduce_fusion
  298.3 183.5 %all-to-all-done.1 = bf16[64,12,4096]{2,1,0:T(8,128)(2,1)} async-done(((bf16[64,12,4096]{2,1,0:T(8,128)(2,1)}), bf16[64,12,4096]{2,1,0:T(8,128)(2,1)}, u32[]{:S(2)}, u32[]{:S(2)}) %all-to-all-start.1) | async-done | bytes 6291488 | tf_op jit(solution)/shard_map/all_to_all | solution.py:43
  481.8 9.9 %reshape.40 = bf16[768,4096]{1,0:T(8,128)(2,1)} reshape(bf16[64,12,4096]{2,1,0:T(8,128)(2,1)} %all-to-all-done.1) | data formatting | bytes 12582912 | tf_op jit(solution)/shard_map/reshape | solution.py:51
  491.6 4.8 convolution_convert_fusion.2
  496.4 0.0 reduce-scatter.2.cloned.1.call-update
  496.5 36.9 %reduce-scatter.2.cloned.1.call-done = bf16[64,512]{1,0:T(8,128)(2,1)} async-done(((bf16[64,4096]{1,0:T(8,128)(2,1)}), bf16[64,512]{1,0:T(8,128)(2,1)}) %reduce-scatter.2.cloned.1.call-update) | async-done | bytes 65552 | tf_op jit(solution)/shard_map/reduce_scatter | solution.py:53
  (3 shorter events, 0.1 us)
Async XLA Ops:
  6.5 259.7 %copy-start = (bf16[1,192,4096]{2,1,0:T(8,128)(2,1)S(1)}, bf16[1,192,4096]{2,1,0:T(8,128)(2,1)}, u32[]{:S(2)}) copy-start(bf16[1,192,4096]{2,1,0:T(8,128)(2,1)} %param.9) | copy-start | bytes 4718596
  250.3 10.1 %copy-start.2 = (bf16[1,192,4096]{2,1,0:T(8,128)(2,1)S(1)}, bf16[1,192,4096]{2,1,0:T(8,128)(2,1)}, u32[]{:S(2)}) copy-start(bf16[1,192,4096]{2,1,0:T(8,128)(2,1)} %param.7) | copy-start | bytes 4718596
  289.5 8.1 %copy-start.1 = (bf16[64,8]{0,1:T(8,128)(2,1)S(1)}, bf16[64,8]{0,1:T(8,128)(2,1)}, u32[]{:S(2)}) copy-start(bf16[64,8]{0,1:T(8,128)(2,1)} %param.11) | copy-start | bytes 3076
  289.5 192.3 %all-to-all-start.1 = ((bf16[64,12,4096]{2,1,0:T(8,128)(2,1)}), bf16[64,12,4096]{2,1,0:T(8,128)(2,1)}, u32[]{:S(2)}, u32[]{:S(2)}) async-start(bf16[64,12,4096]{2,1,0:T(8,128)(2,1)} %reshape.39), calls=%async_computation.1 | async-start | bytes 16777216 | tf_op jit(solution)/shard_map/all_to_all | solution.py:43
  297.6 235.8 %reduce-scatter.2.cloned.1.call-start = ((), (), s32[]{:S(2)}) async-start(), calls=%async_computation.3 | async-start | bytes 589824 | tf_op jit(solution)/shard_map/reduce_scatter | solution.py:53
Sparse Core Ops, SparseCore 0:
  496.6 36.7 reduce-scatter.1
where the time goes:
time: 541 us; the launch traced here: 540 us
  blocking collectives  225 us (42%)
  waiting for transfers between devices  220 us (41%)
  local copies, waits for them, and re-layouts  41.1 us (8%)
  matrix products  28.6 us (5%)
  between operations  13.5 us (2%)
  starting transfers between devices  8.08 us (1%)
    all_to_all x1, blocking collectives, per_device(): lax.all_to_all(placed.astype(jnp.bfloat16).reshape(experts, capacity, who...  198 us
    all_to_all x1, waiting for transfers between devices, per_device(): lax.all_to_all(partial_value.astype(jnp.bfloat16).reshape(arrived.shape),...  184 us
    reduce_scatter x1, waiting for transfers between devices, per_device(): lax.psum_scatter(combined.astype(jnp.bfloat16), 'group', scatter_dimensio...  36.9 us
    all_gather x1, blocking collectives, per_device(): whole_rows = lax.all_gather(tokens, 'group', axis=1, tiled=True)  27.1 us
    dot_general x1, matrix products, per_device(): jnp.dot(hidden, down_weight[0], preferred_element_type=jnp.float32)  13.5 us
  transfers between devices with their start and end apart: 2, of which 2 were waited for; matrix products, arithmetic and copies ran while one was open for 0% of the time, Pallas kernels for 0%

commit v1 on v0

--- a/solution.py
+++ b/solution.py
@@ -20,7 +20,12 @@
     weights = jnp.sum(
         jnp.where(matches, gate_scores[:, :, None].astype(jnp.float32), 0.0), axis=1
     ).astype(jnp.bfloat16)
-    whole_rows = lax.all_gather(tokens, "group", axis=1, tiled=True)
+    amount_of = lax.psum(1, axis_name="group")
+    views = [amount_of if tick == 1 else 1 for tick in range(tokens.ndim)]
+    right_arr = jnp.tile(tokens, views)
+    whole_rows = lax.all_to_all(
+        right_arr, concat_axis=1, split_axis=1, tiled=True, axis_name="group"
+    )
     placed = lax.dot_general(
         selector, whole_rows, (((0,), (0,)), ((), ())), preferred_element_type=jnp.float32
     )

time: 541 us -> 532 us (0.983)
  blocking collectives: 225 us -> 198 us
  waiting for transfers between devices: 220 us -> 230 us
  starting transfers between devices: 8.08 us -> 15.2 us
    all_gather x1 -> x0, blocking collectives: 27.1 us -> none  [per_device(): whole_rows = lax.all_gather(tokens, 'group', axis=1, tiled=True)]
    all_to_all x0 -> x1, waiting for transfers between devices: none -> 13.4 us  [per_device(): lax.all_to_all(right_arr, concat_axis=1, split_axis=1, tiled=True, axis_n...]
    all_to_all x0 -> x1, starting transfers between devices: none -> 7.1 us  [per_device(): lax.all_to_all(right_arr, concat_axis=1, split_axis=1, tiled=True, axis_n...]
  transfers between devices with their start and end apart: 2 -> 3, of which waited for: 2 -> 3; matrix products, arithmetic and copies ran while one was open for 0% -> 1% of each run, Pallas kernels for 0% -> 0%
where the time goes in v1:
time: 532 us; the launch traced here: 531 us
  waiting for transfers between devices  230 us (43%)
  blocking collectives  198 us (37%)
  local copies, waits for them, and re-layouts  42.7 us (8%)
  matrix products  28 us (5%)
  starting transfers between devices  15.2 us (3%)
  between operations  13.5 us (3%)
    all_to_all x1, blocking collectives, per_device(): lax.all_to_all(placed.astype(jnp.bfloat16).reshape(experts, capacity, who...  198 us
    all_to_all x1, waiting for transfers between devices, per_device(): lax.all_to_all(partial_value.astype(jnp.bfloat16).reshape(arrived.shape),...  184 us
    reduce_scatter x1, waiting for transfers between devices, per_device(): lax.psum_scatter(combined.astype(jnp.bfloat16), 'group', scatter_dimensio...  33 us
    all_to_all x1, waiting for transfers between devices, per_device(): lax.all_to_all(right_arr, concat_axis=1, split_axis=1, tiled=True, axis_n...  13.4 us
    dot_general x1, matrix products, per_device(): jnp.dot(hidden, down_weight[0], preferred_element_type=jnp.float32)  13.3 us
  transfers between devices with their start and end apart: 3, of which 3 were waited for; matrix products, arithmetic and copies ran while one was open for 1% of the time, Pallas kernels for 0%

profile of v1, /device:TPU:2, one launch (start us, length us, event | category | flops | bytes accessed | tf_op | source)
XLA Modules:
  0.0 530.7 jit_solution(7177577532529289477)
XLA Ops:
  6.5 0.0 copy-start
  6.5 1.8 tile.2
  8.3 7.1 %all-to-all-start = ((bf16[64,8,512]{2,0,1:T(8,128)(2,1)}), bf16[64,8,512]{2,0,1:T(8,128)(2,1)S(1)}, u32[]{:S(2)}, u32[]{:S(2)}) async-start(bf16[64,8,512]{2,0,1:T(8,128)(2,1)} %tile.2), calls=%async_computation | async-start | bytes 1048576 | tf_op jit(solution)/shard_map/all_to_all | solution.py:26
  15.4 0.8 copy.35
  16.2 0.1 eq.42
  16.3 0.1 eq.38
  16.4 1.2 reduce-window.6
  17.6 0.2 slice_reduce_fusion
  17.9 0.1 fusion.22
  18.0 0.1 reshape.43
  18.1 0.1 copy.38
  18.2 0.7 multiply_add_fusion
  18.9 0.1 copy.39
  19.0 0.5 fusion.5
  19.5 13.4 %all-to-all-done = bf16[64,8,512]{2,0,1:T(8,128)(2,1)S(1)} async-done(((bf16[64,8,512]{2,0,1:T(8,128)(2,1)}), bf16[64,8,512]{2,0,1:T(8,128)(2,1)S(1)}, u32[]{:S(2)}, u32[]{:S(2)}) %all-to-all-start) | async-done | bytes 524320 | tf_op jit(solution)/shard_map/all_to_all | solution.py:26
  33.0 4.6 convolution_convert_fusion
  37.5 9.8 %reshape.44 = bf16[64,12,4096]{2,1,0:T(8,128)(2,1)} reshape(bf16[768,4096]{1,0:T(8,128)(2,1)} %convolution_convert_fusion) | data formatting | bytes 12582912 | tf_op jit(solution)/shard_map/reshape | solution.py:33
  47.3 198.1 %all_to_all.19 = bf16[64,12,4096]{2,1,0:T(8,128)(2,1)} all-to-all(bf16[64,12,4096]{2,1,0:T(8,128)(2,1)} %reshape.44), channel_id=1, replica_groups=mesh['expert'=64,'group'=8] {'expert'}, dimensions={0} | all-to-all | bytes 12582912 | tf_op jit(solution)/shard_map/all_to_all | solution.py:32
  245.4 10.0 %reshape.45 = bf16[768,4096]{1,0:T(8,128)(2,1)} reshape(bf16[64,12,4096]{2,1,0:T(8,128)(2,1)} %all_to_all.19) | data formatting | bytes 12582912 | tf_op jit(solution)/shard_map/reshape | solution.py:39
  255.4 5.4 %fusion.3 = f32[768,192]{0,1:T(8,128)S(1)} fusion(bf16[768,4096]{1,0:T(8,128)(2,1)} %reshape.45, bf16[1,192,4096]{2,1,0:T(8,128)(2,1)} %param.7), kind=kOutput, calls=%fused_computation.6 | convolution fusion | flops 1207959552 | bytes 8454144 | tf_op jit(solution)/shard_map/dot_general | solution.py:40
  260.8 0.0 copy-done
  260.8 13.3 %convolution_convert_fusion.1 = bf16[768,4096]{1,0:T(8,128)(2,1)} fusion(bf16[1,192,4096]{2,1,0:T(8,128)(2,1)S(1)} %copy-done, bf16[768,4096]{1,0:T(8,128)(2,1)} %reshape.45, bf16[1,192,4096]{2,1,0:T(8,128)(2,1)} %param.8, f32[768,192]{0,1:T(8,128)S(1)} %fusion.3), kind=kOutput, calls=%fused_computation.1 | convolution fusion | flops 2419949568 | bytes 16318464 | tf_op jit(solution)/shard_map/dot_general | solution.py:47
  274.1 9.7 %reshape.46 = bf16[64,12,4096]{2,1,0:T(8,128)(2,1)} reshape(bf16[768,4096]{1,0:T(8,128)(2,1)} %convolution_convert_fusion.1) | data formatting | bytes 12582912 | tf_op jit(solution)/shard_map/reshape | solution.py:49
  283.8 0.0 copy-start.1
  283.9 8.1 %all-to-all-start.2 = ((bf16[64,12,4096]{2,1,0:T(8,128)(2,1)}), bf16[64,12,4096]{2,1,0:T(8,128)(2,1)}, u32[]{:S(2)}, u32[]{:S(2)}) async-start(bf16[64,12,4096]{2,1,0:T(8,128)(2,1)} %reshape.46), calls=%async_computation.2 | async-start | bytes 16777216 | tf_op jit(solution)/shard_map/all_to_all | solution.py:48
  291.9 0.0 reduce-scatter.2.cloned.1.call-start
  292.0 0.0 copy-done.1
  292.0 0.1 copy.40
  292.1 0.6 select_reduce_fusion
  292.6 183.5 %all-to-all-done.2 = bf16[64,12,4096]{2,1,0:T(8,128)(2,1)} async-done(((bf16[64,12,4096]{2,1,0:T(8,128)(2,1)}), bf16[64,12,4096]{2,1,0:T(8,128)(2,1)}, u32[]{:S(2)}, u32[]{:S(2)}) %all-to-all-start.2) | async-done | bytes 6291488 | tf_op jit(solution)/shard_map/all_to_all | solution.py:48
  476.2 9.9 %reshape.47 = bf16[768,4096]{1,0:T(8,128)(2,1)} reshape(bf16[64,12,4096]{2,1,0:T(8,128)(2,1)} %all-to-all-done.2) | data formatting | bytes 12582912 | tf_op jit(solution)/shard_map/reshape | solution.py:56
  486.0 4.8 convolution_convert_fusion.2
  490.8 0.0 reduce-scatter.2.cloned.1.call-update
  490.8 33.0 %reduce-scatter.2.cloned.1.call-done = bf16[64,512]{1,0:T(8,128)(2,1)} async-done(((bf16[64,4096]{1,0:T(8,128)(2,1)}), bf16[64,512]{1,0:T(8,128)(2,1)}) %reduce-scatter.2.cloned.1.call-update) | async-done | bytes 65552 | tf_op jit(solution)/shard_map/reduce_scatter | solution.py:58
  (4 shorter events, 0.1 us)
Async XLA Ops:
  6.5 254.3 %copy-start = (bf16[1,192,4096]{2,1,0:T(8,128)(2,1)S(1)}, bf16[1,192,4096]{2,1,0:T(8,128)(2,1)}, u32[]{:S(2)}) copy-start(bf16[1,192,4096]{2,1,0:T(8,128)(2,1)} %param.9) | copy-start | bytes 4718596
  8.3 24.6 %all-to-all-start = ((bf16[64,8,512]{2,0,1:T(8,128)(2,1)}), bf16[64,8,512]{2,0,1:T(8,128)(2,1)S(1)}, u32[]{:S(2)}, u32[]{:S(2)}) async-start(bf16[64,8,512]{2,0,1:T(8,128)(2,1)} %tile.2), calls=%async_computation | async-start | bytes 1048576 | tf_op jit(solution)/shard_map/all_to_all | solution.py:26
  283.8 8.1 %copy-start.1 = (bf16[64,8]{0,1:T(8,128)(2,1)S(1)}, bf16[64,8]{0,1:T(8,128)(2,1)}, u32[]{:S(2)}) copy-start(bf16[64,8]{0,1:T(8,128)(2,1)} %param.11) | copy-start | bytes 3076
  283.9 192.3 %all-to-all-start.2 = ((bf16[64,12,4096]{2,1,0:T(8,128)(2,1)}), bf16[64,12,4096]{2,1,0:T(8,128)(2,1)}, u32[]{:S(2)}, u32[]{:S(2)}) async-start(bf16[64,12,4096]{2,1,0:T(8,128)(2,1)} %reshape.46), calls=%async_computation.2 | async-start | bytes 16777216 | tf_op jit(solution)/shard_map/all_to_all | solution.py:48
  291.9 231.9 %reduce-scatter.2.cloned.1.call-start = ((), (), s32[]{:S(2)}) async-start(), calls=%async_computation.4 | async-start | bytes 589824 | tf_op jit(solution)/shard_map/reduce_scatter | solution.py:58
Sparse Core Ops, SparseCore 0:
  490.9 32.8 reduce-scatter.1
